TPU v7x, 32 devices: a whole 2x2x4 slice. The times are simulated.
32 devices in a mesh: grad: 4 (over y, x), col: 8 (over z, core).
Axes of the slice: x: 2, y: 2, z: 4, core: 2. Of those that a mesh axis runs over, the one named last changes fastest.
Arguments:
- gradient: bfloat16 [16384, 53248], P(('grad', 'col'))
- test_matrix: bfloat16 [16384, 256], P(('grad', 'col')), may hold values from -6 to 6
Outputs:
- low_rank: float32 [16384, 256], P(('grad', 'col'))
- projector: float32 [53248, 256], P('col')
All inputs are finite; a program needn't handle non-finite values.
Results may differ from a plain program's by a relative error of at most 0.008.
Values may be sent and summed in bfloat16 or wider, within the bound.
No kernel may reach another device: no remote copies, remote signals or barrier semaphores. Data moves between devices by JAX's collectives and lax.ppermute only.
A program may use at most 256 MiB of HBM per device.

v0:
```python
import math
import jax
import jax.numpy as jnp
from jax import lax
from jax.sharding import PartitionSpec as P

FF = 53248
POWER = 2


def orthonormal(matrix, reduce_gram):
    partial_gram = lax.dot_general(
        matrix,
        matrix,
        (((0,), (0,)), ((), ())),
        precision=lax.Precision.HIGHEST,
        preferred_element_type=jnp.float32,
    )
    gram = reduce_gram(partial_gram)
    lower_factor = jnp.linalg.cholesky(gram)
    return lax.linalg.triangular_solve(
        lower_factor, matrix, left_side=False, lower=True, transpose_a=True
    )


def gram_over_columns(partial_gram):
    return lax.psum(partial_gram, "col")


def shards(gradient, test_matrix):
    blocks = lax.all_to_all(gradient, "col", split_axis=1, concat_axis=0, tiled=True)

    def add_sketch(row_piece):
        return lax.dot_general(
            blocks, row_piece, (((0,), (0,)), ((), ())), preferred_element_type=jnp.float32
        )

    sketch = add_sketch(lax.all_gather(test_matrix, "col", axis=0, tiled=True))
    for iteration in range(POWER + 1):
        summed = lax.psum(sketch, "grad")
        basis_block = orthonormal(summed, gram_over_columns)
        basis_bf = basis_block.astype(jnp.bfloat16)
        reduced = lax.psum_scatter(
            jnp.dot(blocks, basis_bf, preferred_element_type=jnp.float32),
            "col",
            scatter_dimension=0,
            tiled=True,
        )
        if iteration < POWER:
            reduced_bf = reduced.astype(jnp.bfloat16)
            sketch = add_sketch(lax.all_gather(reduced_bf, "col", axis=0, tiled=True))
    return (reduced, basis_block * math.sqrt(FF))


def solution(mesh):
    return jax.shard_map(
        shards,
        mesh=mesh,
        in_specs=(P(("grad", "col"), None), P(("grad", "col"), None)),
        out_specs=(P(("grad", "col"), None), P("col", None)),
        check_vma=False,
    )
```

profile of v0, /device:TPU:0, one launch (start us, length us, event | category | flops | bytes accessed | tf_op | source)
XLA Modules:
  0.0 2602.8 jit_solution(11232503956803364355)
XLA Ops:
  7.2 70.6 %copy.20 = bf16[512,53248]{0,1:T(8,128)(2,1)} copy(bf16[512,53248]{1,0:T(8,128)(2,1)} %param.5) | data formatting | bytes 109051904 | tf_op args[0]
  77.8 8.8 all-to-all-start
  87.4 1189.5 %all-to-all-done = bf16[512,8,6656]{0,2,1:T(8,128)(2,1)} async-done(((bf16[512,8,6656]{0,2,1:T(8,128)(2,1)}), bf16[512,8,6656]{0,2,1:T(8,128)(2,1)}, u32[]{:S(2)}, u32[]{:S(2)}) %all-to-all-start) | async-done | bytes 54525984 | tf_op jit(solution)/shard_map/all_to_all | solution.py:31
  1276.9 64.6 %copy.21 = bf16[8,512,6656]{2,1,0:T(8,128)(2,1)} copy(bf16[8,512,6656]{1,2,0:T(8,128)(2,1)} %bitcast.1) | data formatting | bytes 109051904 | tf_op jit(solution)/shard_map/all_to_all | solution.py:31
  1341.5 25.8 fusion.41
  1367.7 146.1 %all-reduce.8.cloned.1.call-done = f32[6656,256]{1,0:T(8,128)} async-done(((f32[6656,256]{1,0:T(8,128)}), f32[6656,256]{1,0:T(8,128)}) %all-reduce.8.cloned.1.call-update) | async-done | bytes 6815760 | tf_op jit(solution)/shard_map/psum | solution.py:40
  1513.8 16.6 fusion.42
  1531.0 55.0 %all-reduce.10.cloned.1.call-done = f32[256,256]{0,1:T(8,128)} async-done(((f32[256,256]{0,1:T(8,128)}), f32[256,256]{0,1:T(8,128)}) %all-reduce.10.cloned.1.call-update) | async-done | bytes 262160 | tf_op jit(solution)/shard_map/psum | solution.py:27
  1586.0 1.1 copy.23
  1587.1 1.0 fusion.11
  1588.1 11.7 cholesky.172
  1599.8 9.8 custom-call.15
  1610.2 11.7 cholesky.189
  1624.0 4.2 while.6
  1624.8 1.4 bitcast_dynamic-update-slice_fusion.6
  1626.8 1.4 bitcast_dynamic-update-slice_fusion.6
  1628.9 19.7 custom-call.16
  1648.5 5.2 fusion.7
  1653.7 6.5 convolution_subtract_fusion.2
  1660.3 4.5 fusion.20
  1664.7 24.3 convolution_bitcast_fusion.4
  1689.1 49.1 %reduce-scatter.4.cloned.1.call-done = f32[512,256]{0,1:T(8,128)} async-done(((f32[4096,256]{0,1:T(8,128)}), f32[512,256]{0,1:T(8,128)}) %reduce-scatter.4.cloned.1.call-update) | async-done | bytes 524304 | tf_op jit(solution)/shard_map/reduce_scatter | solution.py:43
  1738.2 1.8 convert_element_type.16
  1740.1 27.8 %all-gather.6.cloned.1.call-done = bf16[4096,256]{0,1:T(8,128)(2,1)} async-done(((bf16[512,256]{0,1:T(8,128)(2,1)}), bf16[4096,256]{0,1:T(8,128)(2,1)}) %all-gather.6.cloned.1.call-update) | async-done | bytes 2097168 | tf_op jit(solution)/shard_map/all_gather | solution.py:51
  1767.9 25.5 convolution_bitcast_fusion.1
  1793.5 146.3 %all-reduce.12.cloned.1.call-done = f32[6656,256]{0,1:T(8,128)} async-done(((f32[6656,256]{0,1:T(8,128)}), f32[6656,256]{0,1:T(8,128)}) %all-reduce.12.cloned.1.call-update) | async-done | bytes 6815760 | tf_op jit(solution)/shard_map/psum | solution.py:40
  1939.8 19.3 fusion.43
  1959.6 55.1 %all-reduce.14.cloned.1.call-done = f32[256,256]{0,1:T(8,128)} async-done(((f32[256,256]{0,1:T(8,128)}), f32[256,256]{0,1:T(8,128)}) %all-reduce.14.cloned.1.call-update) | async-done | bytes 262160 | tf_op jit(solution)/shard_map/psum | solution.py:27
  2014.7 1.1 copy.25
  2016.8 11.7 cholesky.206
  2028.6 9.8 custom-call.17
  2038.9 11.7 cholesky.223
  2053.2 4.2 while.7
  2054.0 1.4 bitcast_dynamic-update-slice_fusion.7
  2056.0 1.4 bitcast_dynamic-update-slice_fusion.7
  2058.1 19.7 custom-call.18
  2077.8 5.2 fusion.5
  2083.0 4.2 convolution_subtract_fusion.1
  2087.2 4.3 fusion.16
  2091.4 24.5 convolution_bitcast_fusion.3
  2116.0 49.1 %reduce-scatter.6.cloned.1.call-done = f32[512,256]{0,1:T(8,128)} async-done(((f32[4096,256]{0,1:T(8,128)}), f32[512,256]{0,1:T(8,128)}) %reduce-scatter.6.cloned.1.call-update) | async-done | bytes 524304 | tf_op jit(solution)/shard_map/reduce_scatter | solution.py:43
  2165.1 1.8 convert_element_type.18
  2167.0 28.0 %all-gather.8.cloned.1.call-done = bf16[4096,256]{0,1:T(8,128)(2,1)} async-done(((bf16[512,256]{0,1:T(8,128)(2,1)}), bf16[4096,256]{0,1:T(8,128)(2,1)}) %all-gather.8.cloned.1.call-update) | async-done | bytes 2097168 | tf_op jit(solution)/shard_map/all_gather | solution.py:51
  2194.9 25.5 convolution_bitcast_fusion
  2220.5 146.3 %all-reduce.16.cloned.1.call-done = f32[6656,256]{0,1:T(8,128)} async-done(((f32[6656,256]{0,1:T(8,128)}), f32[6656,256]{0,1:T(8,128)}) %all-reduce.16.cloned.1.call-update) | async-done | bytes 6815760 | tf_op jit(solution)/shard_map/psum | solution.py:40
  2366.8 19.3 fusion.44
  2386.6 55.1 %all-reduce.18.cloned.1.call-done = f32[256,256]{0,1:T(8,128)} async-done(((f32[256,256]{0,1:T(8,128)}), f32[256,256]{0,1:T(8,128)}) %all-reduce.18.cloned.1.call-update) | async-done | bytes 262160 | tf_op jit(solution)/shard_map/psum | solution.py:27
  2441.8 1.1 copy.28
  2442.9 1.0 fusion.9
  2443.9 11.7 cholesky.240
  2455.6 9.8 custom-call.19
  2465.9 11.7 cholesky.257
  2480.3 4.2 while.8
  2481.1 1.4 bitcast_dynamic-update-slice_fusion.8
  2483.1 1.4 bitcast_dynamic-update-slice_fusion.8
  2485.2 19.7 custom-call.20
  2504.9 5.2 fusion.3
  2510.0 4.2 convolution_subtract_fusion
  2514.2 4.9 fusion.12
  2519.2 25.4 convolution_bitcast_fusion.2
  2544.6 5.4 fusion
  2549.9 8.1 copy.31
  2558.0 35.7 %reduce-scatter.8.cloned.1.call-done = f32[512,256]{0,1:T(8,128)} async-done(((f32[4096,256]{0,1:T(8,128)}), f32[512,256]{0,1:T(8,128)}) %reduce-scatter.8.cloned.1.call-update) | async-done | bytes 524304 | tf_op jit(solution)/shard_map/reduce_scatter | solution.py:43
  2593.7 2.0 copy.30
  (81 shorter events, 14.8 us)
Async XLA Ops:
  77.8 1199.1 %all-to-all-start = ((bf16[512,8,6656]{0,2,1:T(8,128)(2,1)}), bf16[512,8,6656]{0,2,1:T(8,128)(2,1)}, u32[]{:S(2)}, u32[]{:S(2)}) async-start(bf16[512,8,6656]{0,2,1:T(8,128)(2,1)} %bitcast.124), calls=%async_computation | async-start | bytes 109051904 | tf_op jit(solution)/shard_map/all_to_all | solution.py:31
  86.6 1254.9 %all-gather.4.cloned.1.call-start = ((), (), s32[]{:S(2)}) async-start(), calls=%async_computation.4 | async-start | bytes 2359296 | tf_op jit(solution)/shard_map/all_gather | solution.py:38
  87.3 1426.5 %all-reduce.8.cloned.1.call-start = ((), (), s32[]{:S(2)}) async-start(), calls=%async_computation.5 | async-start | bytes 13631488 | tf_op jit(solution)/shard_map/psum | solution.py:40
  1367.4 218.6 %all-reduce.10.cloned.1.call-start = ((), (), s32[]{:S(2)}) async-start(), calls=%async_computation.6 | async-start | bytes 524288 | tf_op jit(solution)/shard_map/psum | solution.py:27
  1530.4 207.8 %reduce-scatter.4.cloned.1.call-start = ((), (), s32[]{:S(2)}) async-start(), calls=%async_computation.7 | async-start | bytes 4718592 | tf_op jit(solution)/shard_map/reduce_scatter | solution.py:43
  1628.2 0.7 copy-start.4
  1648.5 5.2 copy-start
  1689.1 78.8 %all-gather.6.cloned.1.call-start = ((), (), s32[]{:S(2)}) async-start(), calls=%async_computation.8 | async-start | bytes 2359296 | tf_op jit(solution)/shard_map/all_gather | solution.py:51
  1740.0 199.8 %all-reduce.12.cloned.1.call-start = ((), (), s32[]{:S(2)}) async-start(), calls=%async_computation.9 | async-start | bytes 13631488 | tf_op jit(solution)/shard_map/psum | solution.py:40
  1793.4 221.3 %all-reduce.14.cloned.1.call-start = ((), (), s32[]{:S(2)}) async-start(), calls=%async_computation.10 | async-start | bytes 524288 | tf_op jit(solution)/shard_map/psum | solution.py:27
  1959.1 206.0 %reduce-scatter.6.cloned.1.call-start = ((), (), s32[]{:S(2)}) async-start(), calls=%async_computation.11 | async-start | bytes 4718592 | tf_op jit(solution)/shard_map/reduce_scatter | solution.py:43
  2057.4 0.7 copy-start.5
  2077.8 5.2 copy-start.2
  2116.0 79.0 %all-gather.8.cloned.1.call-start = ((), (), s32[]{:S(2)}) async-start(), calls=%async_computation.12 | async-start | bytes 2359296 | tf_op jit(solution)/shard_map/all_gather | solution.py:51
  2166.9 199.9 %all-reduce.16.cloned.1.call-start = ((), (), s32[]{:S(2)}) async-start(), calls=%async_computation.13 | async-start | bytes 13631488 | tf_op jit(solution)/shard_map/psum | solution.py:40
  2220.5 221.3 %all-reduce.18.cloned.1.call-start = ((), (), s32[]{:S(2)}) async-start(), calls=%async_computation.14 | async-start | bytes 524288 | tf_op jit(solution)/shard_map/psum | solution.py:27
  2386.2 207.5 %reduce-scatter.8.cloned.1.call-start = ((), (), s32[]{:S(2)}) async-start(), calls=%async_computation.15 | async-start | bytes 4718592 | tf_op jit(solution)/shard_map/reduce_scatter | solution.py:43
  2484.5 0.7 copy-start.3
  2504.9 5.2 copy-start.1
Sparse Core Ops, SparseCore 0:
  89.0 49.5 all-gather.3
  1367.5 146.2 all-reduce.7
  1530.6 55.4 all-reduce.9
  1689.2 48.9 reduce-scatter.3
  1740.2 27.5 all-gather.5
  1793.5 146.1 all-reduce.11
  1959.2 55.4 all-reduce.13
  2116.1 48.9 reduce-scatter.5
  2167.3 27.6 all-gather.7
  2220.6 146.1 all-reduce.15
  2386.3 55.4 all-reduce.17
  2544.7 48.9 reduce-scatter.7
where the time goes:
time: 2610 us; the launch traced here: 2600 us
  waiting for transfers between devices  1980 us (76%)
  matrix products  252 us (10%)
  other arithmetic  174 us (7%)
  local copies, waits for them, and re-layouts  163 us (6%)
    all_to_all x1, waiting for transfers between devices, shards(): lax.all_to_all(gradient, 'col', split_axis=1, concat_axis=0, tiled=True)  1190 us
    psum x3, waiting for transfers between devices, shards(): summed = lax.psum(sketch, 'grad')  439 us
    psum x3, waiting for transfers between devices, gram_over_columns(): return lax.psum(partial_gram, 'col')  165 us
    reduce_scatter x3, waiting for transfers between devices, shards(): lax.psum_scatter(jnp.dot(blocks, basis_bf, preferred_element_type=jnp.flo...  134 us
    another operation x20, other arithmetic, orthonormal(): lower_factor = jnp.linalg.cholesky(gram)  103 us
    unnamed x15, local copies, waits for them, and re-layouts  82.9 us
    dot_general x3, matrix products, add_sketch(): lax.dot_general(blocks, row_piece, (((0,), (0,)), ((), ())), preferred_el...  76.9 us
    dot_general x3, matrix products, shards(): jnp.dot(blocks, basis_bf, preferred_element_type=jnp.float32)  74.2 us
  transfers between devices with their start and end apart: 13, of which 12 were waited for; matrix products, arithmetic and copies ran while one was open for 3% of the time, Pallas kernels for 0%

commit v1 on v0

--- a/solution.py
+++ b/solution.py
@@ -28,7 +28,10 @@
 
 
 def shards(gradient, test_matrix):
-    blocks = lax.all_to_all(gradient, "col", split_axis=1, concat_axis=0, tiled=True)
+    blocks = jnp.concatenate(
+        lax.all_to_all(jnp.stack(jnp.split(gradient, lax.axis_size("col"), axis=1)), "col", 0, 0),
+        axis=0,
+    )
 
     def add_sketch(row_piece):
         return lax.dot_general(

time: 2610 us -> 2520 us (0.966)
  local copies, waits for them, and re-layouts: 163 us -> 74.9 us
    all_to_all x1 -> x0, local copies, waits for them, and re-layouts: 64.6 us -> none  [shards(): lax.all_to_all(gradient, 'col', split_axis=1, concat_axis=0, tiled=True)]
    all_to_all x1, waiting for transfers between devices: 1190 us -> 1140 us  [shards(): lax.all_to_all(jnp.stack(jnp.split(gradient, lax.axis_size('col'), axis=1...]
    all_gather x1, waiting for transfers between devices: 0.01 us -> 51.2 us  [shards(): sketch = add_sketch(lax.all_gather(test_matrix, 'col', axis=0, tiled=True))]
    unnamed x15 -> x20, local copies, waits for them, and re-layouts: 82.9 us -> 53.5 us
  transfers between devices with their start and end apart: 13 -> 13, of which waited for: 12 -> 13; matrix products, arithmetic and copies ran while one was open for 3% -> 1% of each run, Pallas kernels for 0% -> 0%
where the time goes in v1:
time: 2520 us; the launch traced here: 2510 us
  waiting for transfers between devices  1980 us (79%)
  matrix products  250 us (10%)
  other arithmetic  174 us (7%)
  local copies, waits for them, and re-layouts  74.9 us (3%)
    all_to_all x1, waiting for transfers between devices, shards(): lax.all_to_all(jnp.stack(jnp.split(gradient, lax.axis_size('col'), axis=1...  1140 us
    psum x3, waiting for transfers between devices, shards(): summed = lax.psum(sketch, 'grad')  439 us
    psum x3, waiting for transfers between devices, gram_over_columns(): return lax.psum(partial_gram, 'col')  166 us
    reduce_scatter x3, waiting for transfers between devices, shards(): lax.psum_scatter(jnp.dot(blocks, basis_bf, preferred_element_type=jnp.flo...  134 us
    another operation x20, other arithmetic, orthonormal(): lower_factor = jnp.linalg.cholesky(gram)  103 us
    dot_general x3, matrix products, add_sketch(): lax.dot_general(blocks, row_piece, (((0,), (0,)), ((), ())), preferred_el...  77.5 us
    dot_general x3, matrix products, shards(): jnp.dot(blocks, basis_bf, preferred_element_type=jnp.float32)  71.9 us
    another operation x7, other arithmetic, orthonormal(): lax.linalg.triangular_solve(lower_factor, matrix, left_side=False, lower=...  59.3 us
  transfers between devices with their start and end apart: 13, of which 13 were waited for; matrix products, arithmetic and copies ran while one was open for 1% of the time, Pallas kernels for 0%

profile of v1, /device:TPU:0, one launch (start us, length us, event | category | flops | bytes accessed | tf_op | source)
XLA Modules:
  0.0 2513.4 jit_solution(13879430882355785849)
XLA Ops:
  7.2 6.2 bitcast_dynamic-update-slice_fusion.10
  13.3 6.1 bitcast_dynamic-update-slice_fusion.9
  19.5 6.1 bitcast_dynamic-update-slice_fusion.8
  25.6 6.3 bitcast_dynamic-update-slice_fusion.7
  31.9 6.2 bitcast_dynamic-update-slice_fusion.6
  38.1 6.2 bitcast_dynamic-update-slice_fusion.5
  44.2 6.2 bitcast_dynamic-update-slice_fusion.4
  50.5 6.2 bitcast_dynamic-update-slice_fusion.3
  56.7 8.8 all-to-all-start
  66.3 51.2 %all-gather.4.cloned.1.call-done = bf16[4096,256]{1,0:T(8,128)(2,1)} async-done(((bf16[512,256]{1,0:T(8,128)(2,1)}), bf16[4096,256]{1,0:T(8,128)(2,1)}) %all-gather.4.cloned.1.call-update) | async-done | bytes 2097168 | tf_op jit(solution)/shard_map/all_gather | solution.py:41
  117.5 1138.3 %all-to-all-done = bf16[8,512,6656]{2,1,0:T(8,128)(2,1)} async-done(((bf16[8,512,6656]{2,1,0:T(8,128)(2,1)}), bf16[8,512,6656]{2,1,0:T(8,128)(2,1)}, u32[]{:S(2)}, u32[]{:S(2)}) %all-to-all-start) | async-done | bytes 54525984 | tf_op jit(solution)/shard_map/all_to_all | solution.py:32
  1255.8 25.8 %fusion.44 = f32[6656,256]{1,0:T(8,128)} fusion(bf16[4096,6656]{1,0:T(8,128)(2,1)} %bitcast.8, bf16[4096,256]{1,0:T(8,128)(2,1)} %all-gather.4.cloned.1.call-done), kind=kOutput, calls=%fused_computation.99 | convolution fusion | flops 13958643712 | bytes 63438848 | tf_op jit(solution)/shard_map/dot_general | solution.py:37
  1282.2 145.9 %all-reduce.8.cloned.1.call-done = f32[6656,256]{1,0:T(8,128)} async-done(((f32[6656,256]{1,0:T(8,128)}), f32[6656,256]{1,0:T(8,128)}) %all-reduce.8.cloned.1.call-update) | async-done | bytes 6815760 | tf_op jit(solution)/shard_map/psum | solution.py:43
  1428.1 16.6 fusion.45
  1444.9 55.3 %all-reduce.10.cloned.1.call-done = f32[256,256]{0,1:T(8,128)} async-done(((f32[256,256]{0,1:T(8,128)}), f32[256,256]{0,1:T(8,128)}) %all-reduce.10.cloned.1.call-update) | async-done | bytes 262160 | tf_op jit(solution)/shard_map/psum | solution.py:27
  1502.4 11.7 cholesky.172
  1514.1 9.8 custom-call.15
  1524.4 11.7 cholesky.189
  1538.3 4.4 while.6
  1539.3 1.4 bitcast_dynamic-update-slice_fusion.14
  1541.3 1.4 bitcast_dynamic-update-slice_fusion.14
  1543.4 19.7 custom-call.16
  1563.0 5.2 fusion.10
  1568.2 6.5 convolution_subtract_fusion.2
  1574.8 4.4 fusion.23
  1579.2 23.5 fusion.5
  1602.8 49.1 %reduce-scatter.4.cloned.1.call-done = f32[512,256]{1,0:T(8,128)} async-done(((f32[4096,256]{1,0:T(8,128)}), f32[512,256]{1,0:T(8,128)}) %reduce-scatter.4.cloned.1.call-update) | async-done | bytes 524304 | tf_op jit(solution)/shard_map/reduce_scatter | solution.py:46
  1651.8 1.8 convert_element_type.16
  1653.7 27.8 %all-gather.6.cloned.1.call-done = bf16[4096,256]{1,0:T(8,128)(2,1)} async-done(((bf16[512,256]{1,0:T(8,128)(2,1)}), bf16[4096,256]{1,0:T(8,128)(2,1)}) %all-gather.6.cloned.1.call-update) | async-done | bytes 2097168 | tf_op jit(solution)/shard_map/all_gather | solution.py:54
  1681.5 25.8 %fusion.46 = f32[6656,256]{1,0:T(8,128)} fusion(bf16[4096,6656]{1,0:T(8,128)(2,1)} %bitcast.8, bf16[4096,256]{1,0:T(8,128)(2,1)} %all-gather.6.cloned.1.call-done), kind=kOutput, calls=%fused_computation.101 | convolution fusion | flops 13958643712 | bytes 63438848 | tf_op jit(solution)/shard_map/dot_general | solution.py:37
  1707.4 146.3 %all-reduce.12.cloned.1.call-done = f32[6656,256]{1,0:T(8,128)} async-done(((f32[6656,256]{1,0:T(8,128)}), f32[6656,256]{1,0:T(8,128)}) %all-reduce.12.cloned.1.call-update) | async-done | bytes 6815760 | tf_op jit(solution)/shard_map/psum | solution.py:43
  1853.7 16.6 fusion.47
  1870.8 55.1 %all-reduce.14.cloned.1.call-done = f32[256,256]{0,1:T(8,128)} async-done(((f32[256,256]{0,1:T(8,128)}), f32[256,256]{0,1:T(8,128)}) %all-reduce.14.cloned.1.call-update) | async-done | bytes 262160 | tf_op jit(solution)/shard_map/psum | solution.py:27
  1928.0 11.7 cholesky.206
  1939.8 9.8 custom-call.17
  1950.1 11.7 cholesky.223
  1964.5 4.2 while.7
  1965.2 1.4 bitcast_dynamic-update-slice_fusion.15
  1969.3 19.7 custom-call.18
  1989.0 5.2 fusion.8
  1994.2 6.5 convolution_subtract_fusion.1
  2000.7 4.7 fusion.19
  2005.4 23.5 fusion.4
  2028.9 49.1 %reduce-scatter.6.cloned.1.call-done = f32[512,256]{1,0:T(8,128)} async-done(((f32[4096,256]{1,0:T(8,128)}), f32[512,256]{1,0:T(8,128)}) %reduce-scatter.6.cloned.1.call-update) | async-done | bytes 524304 | tf_op jit(solution)/shard_map/reduce_scatter | solution.py:46
  2078.0 1.8 convert_element_type.18
  2079.9 28.0 %all-gather.8.cloned.1.call-done = bf16[4096,256]{1,0:T(8,128)(2,1)} async-done(((bf16[512,256]{1,0:T(8,128)(2,1)}), bf16[4096,256]{1,0:T(8,128)(2,1)}) %all-gather.8.cloned.1.call-update) | async-done | bytes 2097168 | tf_op jit(solution)/shard_map/all_gather | solution.py:54
  2107.8 25.8 %fusion.48 = f32[6656,256]{1,0:T(8,128)} fusion(bf16[4096,6656]{1,0:T(8,128)(2,1)} %bitcast.8, bf16[4096,256]{1,0:T(8,128)(2,1)} %all-gather.8.cloned.1.call-done), kind=kOutput, calls=%fused_computation.103 | convolution fusion | flops 13958643712 | bytes 63438848 | tf_op jit(solution)/shard_map/dot_general | solution.py:37
  2133.8 146.3 %all-reduce.16.cloned.1.call-done = f32[6656,256]{1,0:T(8,128)} async-done(((f32[6656,256]{1,0:T(8,128)}), f32[6656,256]{1,0:T(8,128)}) %all-reduce.16.cloned.1.call-update) | async-done | bytes 6815760 | tf_op jit(solution)/shard_map/psum | solution.py:43
  2280.0 16.6 fusion.49
  2296.9 55.3 %all-reduce.18.cloned.1.call-done = f32[256,256]{0,1:T(8,128)} async-done(((f32[256,256]{0,1:T(8,128)}), f32[256,256]{0,1:T(8,128)}) %all-reduce.18.cloned.1.call-update) | async-done | bytes 262160 | tf_op jit(solution)/shard_map/psum | solution.py:27
  2354.3 11.7 cholesky.240
  2366.1 9.8 custom-call.19
  2376.4 11.7 cholesky.257
  2390.8 4.0 while.8
  2391.4 1.4 bitcast_dynamic-update-slice_fusion.16
  2393.4 1.4 bitcast_dynamic-update-slice_fusion.16
  2395.5 19.9 custom-call.20
  2415.4 5.2 fusion.6
  2420.6 6.5 convolution_subtract_fusion
  2427.1 5.0 fusion.15
  2432.1 24.9 fusion.2
  2457.0 5.4 fusion
  2462.4 8.1 copy.10
  2470.5 35.7 %reduce-scatter.8.cloned.1.call-done = f32[512,256]{1,0:T(8,128)} async-done(((f32[4096,256]{1,0:T(8,128)}), f32[512,256]{1,0:T(8,128)}) %reduce-scatter.8.cloned.1.call-update) | async-done | bytes 524304 | tf_op jit(solution)/shard_map/reduce_scatter | solution.py:46
  (86 shorter events, 21.0 us)
Async XLA Ops:
  56.7 1199.1 %all-to-all-start = ((bf16[8,512,6656]{2,1,0:T(8,128)(2,1)}), bf16[8,512,6656]{2,1,0:T(8,128)(2,1)}, u32[]{:S(2)}, u32[]{:S(2)}) async-start(bf16[8,512,6656]{2,1,0:T(8,128)(2,1)} %bitcast_dynamic-update-slice_fusion.3), calls=%async_computation | async-start | bytes 109051904 | tf_op jit(solution)/shard_map/all_to_all | solution.py:32
  65.5 52.0 %all-gather.4.cloned.1.call-start = ((), (), s32[]{:S(2)}) async-start(), calls=%async_computation.4 | async-start | bytes 2359296 | tf_op jit(solution)/shard_map/all_gather | solution.py:41
  66.2 1361.9 %all-reduce.8.cloned.1.call-start = ((), (), s32[]{:S(2)}) async-start(), calls=%async_computation.5 | async-start | bytes 13631488 | tf_op jit(solution)/shard_map/psum | solution.py:43
  1281.6 218.7 %all-reduce.10.cloned.1.call-start = ((), (), s32[]{:S(2)}) async-start(), calls=%async_computation.6 | async-start | bytes 524288 | tf_op jit(solution)/shard_map/psum | solution.py:27
  1444.7 207.1 %reduce-scatter.4.cloned.1.call-start = ((), (), s32[]{:S(2)}) async-start(), calls=%async_computation.7 | async-start | bytes 4718592 | tf_op jit(solution)/shard_map/reduce_scatter | solution.py:46
  1542.7 0.7 copy-start.4
  1563.0 5.2 copy-start
  1602.7 78.8 %all-gather.6.cloned.1.call-start = ((), (), s32[]{:S(2)}) async-start(), calls=%async_computation.8 | async-start | bytes 2359296 | tf_op jit(solution)/shard_map/all_gather | solution.py:54
  1653.6 200.1 %all-reduce.12.cloned.1.call-start = ((), (), s32[]{:S(2)}) async-start(), calls=%async_computation.9 | async-start | bytes 13631488 | tf_op jit(solution)/shard_map/psum | solution.py:43
  1707.4 218.5 %all-reduce.14.cloned.1.call-start = ((), (), s32[]{:S(2)}) async-start(), calls=%async_computation.10 | async-start | bytes 524288 | tf_op jit(solution)/shard_map/psum | solution.py:27
  1870.3 207.7 %reduce-scatter.6.cloned.1.call-start = ((), (), s32[]{:S(2)}) async-start(), calls=%async_computation.11 | async-start | bytes 4718592 | tf_op jit(solution)/shard_map/reduce_scatter | solution.py:46
  1968.6 0.7 copy-start.5
  1989.0 5.2 copy-start.2
  2028.9 78.9 %all-gather.8.cloned.1.call-start = ((), (), s32[]{:S(2)}) async-start(), calls=%async_computation.12 | async-start | bytes 2359296 | tf_op jit(solution)/shard_map/all_gather | solution.py:54
  2079.8 200.2 %all-reduce.16.cloned.1.call-start = ((), (), s32[]{:S(2)}) async-start(), calls=%async_computation.13 | async-start | bytes 13631488 | tf_op jit(solution)/shard_map/psum | solution.py:43
  2133.7 218.5 %all-reduce.18.cloned.1.call-start = ((), (), s32[]{:S(2)}) async-start(), calls=%async_computation.14 | async-start | bytes 524288 | tf_op jit(solution)/shard_map/psum | solution.py:27
  2296.7 209.5 %reduce-scatter.8.cloned.1.call-start = ((), (), s32[]{:S(2)}) async-start(), calls=%async_computation.15 | async-start | bytes 4718592 | tf_op jit(solution)/shard_map/reduce_scatter | solution.py:46
  2394.8 0.7 copy-start.3
  2415.4 5.2 copy-start.1
Sparse Core Ops, SparseCore 0:
  67.9 49.5 all-gather.3
  1281.7 146.3 all-reduce.7
  1444.8 55.4 all-reduce.9
  1602.8 48.9 reduce-scatter.3
  1653.9 27.6 all-gather.5
  1707.5 146.1 all-reduce.11
  1870.5 55.4 all-reduce.13
  2029.0 48.9 reduce-scatter.5
  2080.2 27.5 all-gather.7
  2133.8 146.1 all-reduce.15
  2296.8 55.4 all-reduce.17
  2457.1 48.9 reduce-scatter.7
